TPU v7x, 32 devices: a whole 2x2x4 slice. The times are simulated.
32 devices in a mesh: dp: 4 (over z), space: 4 (over x, core), rep: 2 (over y).
Axes of the slice: x: 2, y: 2, z: 4, core: 2. Of those that a mesh axis runs over, the one named last changes fastest.
Arguments:
- frames: bfloat16 [6, 8, 32, 32, 512], P(None, ('dp', 'rep'), 'space'), may hold values from -6 to 6
- membrane: bfloat16 [8, 32, 32, 512], P(('dp', 'rep'), 'space'), may hold values from -6 to 6
- cotangent: bfloat16 [6, 8, 32, 32, 512], P(None, ('dp', 'rep'), 'space'), may hold values from -6 to 6
- master: float32 [4608, 512], P('dp'), may hold values from -0.09375 to 0.09375
- moment: float32 [4608, 512], P('dp'), may hold values from -4 to 4
- second: float32 [4608, 512], P('dp'), may hold values from 0.05 to 5
Outputs:
- grad_input: bfloat16 [6, 8, 32, 32, 512], P(None, ('dp', 'rep'), 'space')
- membrane_grad: float32 [8, 32, 32, 512], P(('dp', 'rep'), 'space')
- weight_grad: float32 [4608, 512], P('dp')
- new_moment: float32 [4608, 512], P('dp')
- new_second: float32 [4608, 512], P('dp')
- update: float32 [4608, 512], P('dp')
All inputs are finite; a program needn't handle non-finite values.
Results may differ from a plain program's by a relative error of at most 0.003.
Values may be sent and summed in bfloat16 or wider, within the bound.
No kernel may reach another device: no remote copies, remote signals or barrier semaphores. Data moves between devices by JAX's collectives and lax.ppermute only.
A program may use at most 192 MiB of HBM per device.

v0:
```python
import math
import jax
import jax.numpy as jnp
from jax import lax
from jax.sharding import PartitionSpec as P


def extended(x, sides, width):
    for axis, dim in sides:
        peers, length = (lax.axis_size(axis), x.shape[dim])
        up = [(i, (i + 1) % peers) for i in range(peers - 1)]
        down = [(j, i) for i, j in up]
        last = lax.slice_in_dim(x, length - width, length, axis=dim)
        first = lax.slice_in_dim(x, 0, width, axis=dim)
        before = lax.ppermute(last, axis, up)
        after = lax.ppermute(first, axis, down)
        x = jnp.concatenate([before, x, after], axis=dim)
    return x


def surrogate(potential):
    return 1.0 / (1.0 + (math.pi * (potential - 1.0)) ** 2)


def offsets_list():
    return [(row_shift, col_shift) for row_shift in (-1, 0, 1) for col_shift in (-1, 0, 1)]


def on_device(frames, membrane, cotangent, master, moment, second):
    steps_count, samples, rows, cols, chans = frames.shape
    weights = lax.all_gather(master.astype(jnp.bfloat16), "dp", axis=0, tiled=True)
    stacked = jnp.concatenate([membrane[None], frames], axis=0)
    rimmed = extended(stacked, (("space", 2),), 1)
    voltage = rimmed[0].astype(jnp.float32)
    potentials = []
    fired = []
    for position in range(steps_count):
        potential = 0.5 * voltage + rimmed[position + 1].astype(jnp.float32)
        spikes = jnp.where(potential >= 1.0, jnp.float32(1.0), jnp.float32(0.0))
        voltage = potential - spikes
        potentials.append(potential[:, 1:-1])
        fired.append(spikes)
    potential_all = jnp.stack(potentials)
    spike_all = jnp.stack(fired).astype(jnp.bfloat16)
    col_pad = ((0, 0), (0, 0), (0, 0), (1, 1), (0, 0))
    spike_pad = jnp.pad(spike_all, col_pad)
    grad_rim = extended(cotangent, (("space", 2),), 1)
    grad_pad = jnp.pad(grad_rim, col_pad)
    spike_cols = jnp.concatenate(
        [spike_pad[:, :, 1 + a : 1 + a + rows, 1 + b : 1 + b + cols] for a, b in offsets_list()],
        axis=-1,
    ).reshape(-1, 9 * chans)
    grad_cols = jnp.concatenate(
        [grad_pad[:, :, 1 - a : 1 - a + rows, 1 - b : 1 - b + cols] for a, b in offsets_list()],
        axis=-1,
    ).reshape(-1, 9, chans)
    grad_flat = cotangent.reshape(-1, chans)
    weight_local = lax.dot_general(
        spike_cols, grad_flat, (((0,), (0,)), ((), ())), preferred_element_type=jnp.float32
    )
    dspikes = jnp.einsum(
        "nkd,kcd->nc",
        grad_cols,
        weights.reshape(9, chans, chans),
        preferred_element_type=jnp.float32,
    )
    dspikes = dspikes.reshape(steps_count, samples, rows, cols, chans)
    carried = jnp.zeros((samples, rows, cols, chans), jnp.float32)
    outs = [None] * steps_count
    for position in reversed(range(steps_count)):
        carried = dspikes[position] * surrogate(potential_all[position]) + 0.5 * carried
        outs[position] = (cotangent[position].astype(jnp.float32) + carried).astype(jnp.bfloat16)
    grad_input = jnp.stack(outs)
    membrane_grad = 0.5 * carried
    data_count = lax.axis_size("dp")
    total_cells = samples * data_count * lax.axis_size("rep") * rows * lax.axis_size("space") * cols
    shard_part = lax.psum_scatter(weight_local, "dp", scatter_dimension=0, tiled=True)
    summed = lax.psum(shard_part, ("space", "rep"))
    weight_grad = summed * (1.0 / math.sqrt(steps_count * total_cells))
    new_moment = 0.9 * moment + 0.1 * weight_grad
    new_second = 0.95 * second + 0.05 * weight_grad * weight_grad
    update = new_moment / (jnp.sqrt(new_second) + 1e-08)
    return (grad_input, membrane_grad, weight_grad, new_moment, new_second, update)


def solution(mesh):
    return jax.shard_map(
        on_device,
        mesh=mesh,
        in_specs=(
            P(None, ("dp", "rep"), "space", None, None),
            P(("dp", "rep"), "space", None, None),
            P(None, ("dp", "rep"), "space", None, None),
            P("dp", None),
            P("dp", None),
            P("dp", None),
        ),
        out_specs=(
            P(None, ("dp", "rep"), "space", None, None),
            P(("dp", "rep"), "space", None, None),
            P("dp", None),
            P("dp", None),
            P("dp", None),
            P("dp", None),
        ),
        check_vma=False,
    )
```

profile of v0, /device:TPU:0, one launch (start us, length us, event | category | flops | bytes accessed | tf_op | source)
XLA Modules:
  0.0 351.5 jit_solution(18133478292274602957)
XLA Ops:
  7.2 1.1 pad_maximum_fusion.4
  8.3 1.3 collective-permute-start.3
  9.6 3.2 collective-permute-start.2
  12.8 2.8 convert_element_type.357
  15.7 1.8 pad_maximum_fusion
  17.9 0.4 fusion.80
  18.3 0.5 fusion.82
  19.0 0.3 fusion.74
  19.4 0.5 fusion.16
  20.0 0.7 fusion.17
  20.7 0.7 fusion.18
  21.6 0.7 fusion.19
  22.3 0.8 fusion.20
  23.2 0.7 fusion.21
  23.9 0.7 copy-done
  24.6 10.2 %fusion.4 = f32[4608,512]{1,0:T(8,128)} fusion(bf16[6,1,8,32,4608]{4,3,2,0,1:T(8,128)(2,1)S(1)} %fusion.21, bf16[6,1,8,32,512]{4,3,2,1,0:T(8,128)(2,1)S(1)} %copy-done), kind=kOutput, calls=%fused_computation.4 | convolution fusion | flops 7247757312 | bytes 25165824 | tf_op jit(solution)/shard_map/dot_general | solution.py:58
  34.8 1.1 fusion.104
  35.9 1.3 collective-permute-start.1
  37.2 5.5 %collective-permute-start = (bf16[6,1,1,32,512]{4,3,2,1,0:T(8,128)(2,1)S(1)}, bf16[6,1,1,32,512]{4,3,2,1,0:T(8,128)(2,1)S(1)}, u32[]{:S(2)}, u32[]{:S(2)}) collective-permute-start(bf16[6,1,1,32,512]{4,3,2,1,0:T(8,128)(2,1)S(1)} %get-tuple-element.29), channel_id=1, source_target_pairs={{0,2},{2,4},{4,6},{1,3},{3,5},{5,7},{8,10},{10,12},{12,14},{9,11},... | collective-permute-start | bytes 589832 | tf_op jit(solution)/shard_map/ppermute | solution.py:15
  42.7 0.8 collective-permute-done
  43.5 2.3 fusion.15
  45.9 1.7 slice_dynamic-update-slice_fusion.8
  47.5 1.4 fusion.23
  49.0 1.4 slice_dynamic-update-slice_fusion.7
  50.4 2.1 slice_dynamic-update-slice_fusion.6
  52.5 1.4 constant_dynamic-update-slice_fusion
  53.8 1.4 slice_dynamic-update-slice_fusion.5
  55.2 2.0 slice_dynamic-update-slice_fusion.4
  57.2 1.4 fusion.22
  58.6 1.4 slice_dynamic-update-slice_fusion.3
  60.0 26.6 %reshape.515 = bf16[1536,9,512]{2,1,0:T(8,128)(2,1)} reshape(bf16[6,1,8,32,4608]{4,3,2,1,0:T(8,128)(2,1)} %slice_dynamic-update-slice_fusion.3) | data formatting | bytes 28311552 | tf_op jit(solution)/shard_map/reshape | solution.py:56
  86.6 1.0 fusion.73
  87.6 0.9 convert_bitcast_fusion.1
  88.6 1.8 fusion.28
  90.4 17.5 %all-gather.2.cloned.1.call-done = bf16[4608,512]{1,0:T(8,128)(2,1)} async-done(((bf16[1152,512]{1,0:T(8,128)(2,1)}), bf16[4608,512]{1,0:T(8,128)(2,1)}) %all-gather.2.cloned.1.call-update) | async-done | bytes 4718608 | tf_op jit(solution)/shard_map/all_gather | solution.py:31
  107.9 25.8 %fusion.8 = f32[1536,512]{1,0:T(8,128)S(1)} fusion(bf16[9,512,512]{2,1,0:T(8,128)(2,1)} %bitcast.158, bf16[1536,9,512]{2,1,0:T(8,128)(2,1)} %reshape.515), kind=kOutput, calls=%fused_computation.8 | convolution fusion | flops 7247757312 | bytes 22020096 | tf_op jit(solution)/shard_map/nkd,kcd->nc/dot_general | solution.py:61
  133.8 0.3 fusion.103
  134.1 0.7 copy-done.4
  135.8 1.7 broadcast_multiply_fusion.1
  137.6 0.8 fusion.85
  138.3 131.7 %reduce-scatter.2.cloned.1.call-done = f32[1152,512]{1,0:T(8,128)} async-done(((f32[4608,512]{1,0:T(8,128)}), f32[1152,512]{1,0:T(8,128)}) %reduce-scatter.2.cloned.1.call-update) | async-done | bytes 2359312 | tf_op jit(solution)/shard_map/reduce_scatter | solution.py:77
  270.1 2.2 fusion.87
  272.3 0.8 fusion.89
  273.1 0.8 fusion.91
  273.9 0.9 fusion.93
  274.8 0.8 fusion.95
  275.6 61.5 %all-reduce.4.cloned.1.call-done = f32[1152,512]{1,0:T(8,128)} async-done(((f32[1152,512]{1,0:T(8,128)}), f32[1152,512]{1,0:T(8,128)}) %all-reduce.4.cloned.1.call-update) | async-done | bytes 2359312 | tf_op jit(solution)/shard_map/psum | solution.py:78
  337.1 7.9 %add_divide_fusion = (f32[1152,512]{1,0:T(8,128)}, f32[1152,512]{1,0:T(8,128)}, f32[1152,512]{1,0:T(8,128)}, f32[1152,512]{1,0:T(8,128)}) fusion(f32[1152,512]{1,0:T(8,128)} %all-reduce.4.cloned.1.call-done, f32[1152,512]{1,0:T(8,128)} %param.11, f32[1152,512]{1,0:T(8,128)} %param.10), kind=kLoop, calls=%fused_computation.14 | loop fusion | flops 5898240 | bytes 16515072 | tf_op jit(solution)/shard_map/div | solution.py:82
  (39 shorter events, 2.1 us)
Async XLA Ops:
  7.2 100.7 %all-gather.2.cloned.1.call-start = ((), (), s32[]{:S(2)}) async-start(), calls=%async_computation.1 | async-start | bytes 5898240 | tf_op jit(solution)/shard_map/all_gather | solution.py:31
  8.3 7.4 %collective-permute-start.3 = (bf16[7,1,1,32,512]{4,3,2,1,0:T(8,128)(2,1)S(1)}, bf16[7,1,1,32,512]{4,3,2,1,0:T(8,128)(2,1)S(1)}, u32[]{:S(2)}, u32[]{:S(2)}) collective-permute-start(bf16[7,1,1,32,512]{4,3,2,1,0:T(8,128)(2,1)S(1)} %get-tuple-element.28), channel_id=1, source_target_pairs={{2,0},{4,2},{6,4},{3,1},{5,3},{7,5},{10,8},{12,10},{14,12},{11,9},... | collective-permute-start | bytes 688136 | tf_op jit(solution)/shard_map/ppermute | solution.py:16
  9.6 6.1 %copy-start.12 = (bf16[1,8,32,512]{3,2,1,0:T(8,128)(2,1)S(1)}, bf16[1,8,32,512]{3,2,1,0:T(8,128)(2,1)}, u32[]{:S(2)}) copy-start(bf16[1,8,32,512]{3,2,1,0:T(8,128)(2,1)} %param.7) | copy-start | bytes 786436
  9.6 6.1 %collective-permute-start.2 = (bf16[7,1,1,32,512]{4,3,2,1,0:T(8,128)(2,1)S(1)}, bf16[7,1,1,32,512]{4,3,2,1,0:T(8,128)(2,1)S(1)}, u32[]{:S(2)}, u32[]{:S(2)}) collective-permute-start(bf16[7,1,1,32,512]{4,3,2,1,0:T(8,128)(2,1)S(1)} %get-tuple-element.27), channel_id=1, source_target_pairs={{0,2},{2,4},{4,6},{1,3},{3,5},{5,7},{8,10},{10,12},{12,14},{9,11},... | collective-permute-start | bytes 688136 | tf_op jit(solution)/shard_map/ppermute | solution.py:15
  15.6 254.4 %reduce-scatter.2.cloned.1.call-start = ((), (), s32[]{:S(2)}) async-start(), calls=%async_computation.2 | async-start | bytes 11796480 | tf_op jit(solution)/shard_map/reduce_scatter | solution.py:77
  23.2 1.4 copy-start
  34.8 302.3 %all-reduce.4.cloned.1.call-start = ((), (), s32[]{:S(2)}) async-start(), calls=%async_computation.3 | async-start | bytes 4718592 | tf_op jit(solution)/shard_map/psum | solution.py:78
  35.9 6.8 %collective-permute-start.1 = (bf16[6,1,1,32,512]{4,3,2,1,0:T(8,128)(2,1)S(1)}, bf16[6,1,1,32,512]{4,3,2,1,0:T(8,128)(2,1)S(1)}, u32[]{:S(2)}, u32[]{:S(2)}) collective-permute-start(bf16[6,1,1,32,512]{4,3,2,1,0:T(8,128)(2,1)S(1)} %get-tuple-element.30), channel_id=1, source_target_pairs={{2,0},{4,2},{6,4},{3,1},{5,3},{7,5},{10,8},{12,10},{14,12},{11,9},... | collective-permute-start | bytes 589832 | tf_op jit(solution)/shard_map/ppermute | solution.py:16
  37.2 6.3 %collective-permute-start = (bf16[6,1,1,32,512]{4,3,2,1,0:T(8,128)(2,1)S(1)}, bf16[6,1,1,32,512]{4,3,2,1,0:T(8,128)(2,1)S(1)}, u32[]{:S(2)}, u32[]{:S(2)}) collective-permute-start(bf16[6,1,1,32,512]{4,3,2,1,0:T(8,128)(2,1)S(1)} %get-tuple-element.29), channel_id=1, source_target_pairs={{0,2},{2,4},{4,6},{1,3},{3,5},{5,7},{8,10},{10,12},{12,14},{9,11},... | collective-permute-start | bytes 589832 | tf_op jit(solution)/shard_map/ppermute | solution.py:15
  45.8 1.7 copy-start.1
  133.7 1.1 copy-start.4
  133.7 1.3 copy-start.6
  133.7 1.5 copy-start.7
  133.8 1.7 copy-start.8
  133.8 1.8 copy-start.9
  133.8 2.0 copy-start.10
  135.8 1.7 copy-start.2
  270.1 2.3 copy-start.3
  270.1 3.0 copy-start.11
  270.1 3.8 %copy-start.5 = (f32[1,10,32,512]{3,2,1,0:T(8,128)S(1)}, f32[1,10,32,512]{3,2,1,0:T(8,128)}, u32[]{:S(2)}) copy-start(f32[1,10,32,512]{3,2,1,0:T(8,128)} %get-tuple-element.17) | copy-start | bytes 1966084
Sparse Core Ops, SparseCore 0:
  15.8 92.1 all-gather.1
  110.3 159.7 reduce-scatter.1
  273.3 63.7 all-reduce.3
where the time goes:
time: 353 us; the launch traced here: 352 us
  waiting for transfers between devices  212 us (60%)
  local copies, waits for them, and re-layouts  46.2 us (13%)
  matrix products  36 us (10%)
  other arithmetic  32.3 us (9%)
  between operations  14.1 us (4%)
  starting transfers between devices  11.3 us (3%)
    reduce_scatter x1, waiting for transfers between devices, on_device(): lax.psum_scatter(weight_local, 'dp', scatter_dimension=0, tiled=True)  132 us
    psum x1, waiting for transfers between devices, on_device(): summed = lax.psum(shard_part, ('space', 'rep'))  61.5 us
    reshape x1, local copies, waits for them, and re-layouts, on_device(): grad_cols = jnp.concatenate([grad_pad[:, :, 1 - a:1 - a + rows, 1 - b:1 -...  26.6 us
    dot_general x1, matrix products, on_device(): jnp.einsum('nkd,kcd->nc', grad_cols, weights.reshape(9, chans, chans), pr...  25.8 us
    all_gather x1, waiting for transfers between devices, on_device(): lax.all_gather(master.astype(jnp.bfloat16), 'dp', axis=0, tiled=True)  17.5 us
    unnamed x40, local copies, waits for them, and re-layouts  16.1 us
    dot_general x1, matrix products, on_device(): lax.dot_general(spike_cols, grad_flat, (((0,), (0,)), ((), ())), preferre...  10.2 us
    unnamed x12, other arithmetic  9.82 us
  transfers between devices with their start and end apart: 7, of which 4 were waited for; matrix products, arithmetic and copies ran while one was open for 29% of the time, Pallas kernels for 0%

commit v1 on v0

--- a/solution.py
+++ b/solution.py
@@ -75,7 +75,7 @@
     data_count = lax.axis_size("dp")
     total_cells = samples * data_count * lax.axis_size("rep") * rows * lax.axis_size("space") * cols
     shard_part = lax.psum_scatter(weight_local, "dp", scatter_dimension=0, tiled=True)
-    summed = lax.psum(shard_part, ("space", "rep"))
+    summed = lax.psum(lax.psum(shard_part, "rep"), "space")
     weight_grad = summed * (1.0 / math.sqrt(steps_count * total_cells))
     new_moment = 0.9 * moment + 0.1 * weight_grad
     new_second = 0.95 * second + 0.05 * weight_grad * weight_grad

time: 353 us -> 435 us (1.23)
  waiting for transfers between devices: 212 us -> 294 us
    all_gather x1, waiting for transfers between devices: 17.5 us -> 92.4 us  [on_device(): lax.all_gather(master.astype(jnp.bfloat16), 'dp', axis=0, tiled=True)]
    psum x1 -> x2, waiting for transfers between devices: 61.5 us -> 91.7 us  [on_device(): summed = lax.psum(lax.psum(shard_part, 'rep'), 'space')]
    reduce_scatter x1, waiting for transfers between devices: 132 us -> 108 us  [on_device(): lax.psum_scatter(weight_local, 'dp', scatter_dimension=0, tiled=True)]
    unnamed x40 -> x42, local copies, waits for them, and re-layouts: 16.1 us -> 16 us
  transfers between devices with their start and end apart: 7 -> 8, of which waited for: 4 -> 6; matrix products, arithmetic and copies ran while one was open for 29% -> 19% of each run, Pallas kernels for 0% -> 0%
where the time goes in v1:
time: 435 us; the launch traced here: 434 us
  waiting for transfers between devices  294 us (68%)
  local copies, waits for them, and re-layouts  46.2 us (11%)
  matrix products  35.8 us (8%)
  other arithmetic  31 us (7%)
  between operations  14.1 us (3%)
  starting transfers between devices  12.9 us (3%)
    reduce_scatter x1, waiting for transfers between devices, on_device(): lax.psum_scatter(weight_local, 'dp', scatter_dimension=0, tiled=True)  108 us
    all_gather x1, waiting for transfers between devices, on_device(): lax.all_gather(master.astype(jnp.bfloat16), 'dp', axis=0, tiled=True)  92.4 us
    psum x2, waiting for transfers between devices, on_device(): summed = lax.psum(lax.psum(shard_part, 'rep'), 'space')  91.7 us
    reshape x1, local copies, waits for them, and re-layouts, on_device(): grad_cols = jnp.concatenate([grad_pad[:, :, 1 - a:1 - a + rows, 1 - b:1 -...  26.6 us
    dot_general x1, matrix products, on_device(): jnp.einsum('nkd,kcd->nc', grad_cols, weights.reshape(9, chans, chans), pr...  25.6 us
    unnamed x42, local copies, waits for them, and re-layouts  16 us
    dot_general x1, matrix products, on_device(): lax.dot_general(spike_cols, grad_flat, (((0,), (0,)), ((), ())), preferre...  10.2 us
    ppermute x2, starting transfers between devices, extended(): before = lax.ppermute(last, axis, up)  10.2 us
  transfers between devices with their start and end apart: 8, of which 6 were waited for; matrix products, arithmetic and copies ran while one was open for 19% of the time, Pallas kernels for 0%

profile of v1, /device:TPU:0, one launch (start us, length us, event | category | flops | bytes accessed | tf_op | source)
XLA Modules:
  0.0 433.8 jit_solution(415623557436342763)
XLA Ops:
  7.2 1.2 pad_maximum_fusion.4
  8.4 1.3 collective-permute-start.3
  9.7 3.0 collective-permute-start.2
  12.8 1.1 collective-permute-done.2
  13.9 0.4 pad_maximum_fusion
  14.7 0.4 fusion.80
  15.1 0.5 fusion.82
  16.1 0.5 fusion.16
  16.7 0.7 fusion.17
  17.4 0.7 fusion.18
  18.3 0.7 fusion.19
  19.0 0.7 fusion.20
  19.9 0.7 fusion.21
  20.6 0.7 copy-done
  21.3 10.2 %fusion.4 = f32[4608,512]{1,0:T(8,128)} fusion(bf16[6,1,8,32,4608]{4,3,2,0,1:T(8,128)(2,1)S(1)} %fusion.21, bf16[6,1,8,32,512]{4,3,2,1,0:T(8,128)(2,1)S(1)} %copy-done), kind=kOutput, calls=%fused_computation.4 | convolution fusion | flops 7247757312 | bytes 25165824 | tf_op jit(solution)/shard_map/dot_general | solution.py:58
  31.6 2.8 convert_element_type.357
  34.5 1.1 fusion.104
  35.5 1.3 collective-permute-start.1
  36.8 7.1 %collective-permute-start = (bf16[6,1,1,32,512]{4,3,2,1,0:T(8,128)(2,1)S(1)}, bf16[6,1,1,32,512]{4,3,2,1,0:T(8,128)(2,1)S(1)}, u32[]{:S(2)}, u32[]{:S(2)}) collective-permute-start(bf16[6,1,1,32,512]{4,3,2,1,0:T(8,128)(2,1)S(1)} %get-tuple-element.29), channel_id=1, source_target_pairs={{0,2},{2,4},{4,6},{1,3},{3,5},{5,7},{8,10},{10,12},{12,14},{9,11},... | collective-permute-start | bytes 589832 | tf_op jit(solution)/shard_map/ppermute | solution.py:15
  44.0 0.8 collective-permute-done
  44.8 2.4 fusion.15
  47.2 1.7 slice_dynamic-update-slice_fusion.8
  48.9 1.5 fusion.23
  50.4 1.4 slice_dynamic-update-slice_fusion.7
  51.8 2.0 slice_dynamic-update-slice_fusion.6
  53.7 1.4 constant_dynamic-update-slice_fusion
  55.1 1.4 slice_dynamic-update-slice_fusion.5
  56.6 2.0 slice_dynamic-update-slice_fusion.4
  58.5 1.4 fusion.22
  59.9 1.5 slice_dynamic-update-slice_fusion.3
  61.4 26.6 %reshape.515 = bf16[1536,9,512]{2,1,0:T(8,128)(2,1)} reshape(bf16[6,1,8,32,4608]{4,3,2,1,0:T(8,128)(2,1)} %slice_dynamic-update-slice_fusion.3) | data formatting | bytes 28311552 | tf_op jit(solution)/shard_map/reshape | solution.py:56
  88.0 0.9 fusion.73
  88.9 0.9 convert_bitcast_fusion.1
  89.8 1.8 fusion.28
  91.7 107.8 %reduce-scatter.2.cloned.1.call-done = f32[1152,512]{1,0:T(8,128)} async-done(((f32[4608,512]{1,0:T(8,128)}), f32[1152,512]{1,0:T(8,128)}) %reduce-scatter.2.cloned.1.call-update) | async-done | bytes 2359312 | tf_op jit(solution)/shard_map/reduce_scatter | solution.py:77
  199.6 92.4 %all-gather.2.cloned.1.call-done = bf16[4608,512]{1,0:T(8,128)(2,1)} async-done(((bf16[1152,512]{1,0:T(8,128)(2,1)}), bf16[4608,512]{1,0:T(8,128)(2,1)}) %all-gather.2.cloned.1.call-update) | async-done | bytes 4718608 | tf_op jit(solution)/shard_map/all_gather | solution.py:31
  291.9 25.6 %fusion.8 = f32[1536,512]{1,0:T(8,128)S(1)} fusion(bf16[9,512,512]{2,1,0:T(8,128)(2,1)} %bitcast.158, bf16[1536,9,512]{2,1,0:T(8,128)(2,1)} %reshape.515), kind=kOutput, calls=%fused_computation.8 | convolution fusion | flops 7247757312 | bytes 22020096 | tf_op jit(solution)/shard_map/nkd,kcd->nc/dot_general | solution.py:61
  317.9 0.7 copy-done.5
  319.6 1.7 broadcast_multiply_fusion.1
  321.3 0.8 fusion.85
  322.1 39.2 %all-reduce.5.cloned.1.call-done = f32[1152,512]{1,0:T(8,128)} async-done(((f32[1152,512]{1,0:T(8,128)}), f32[1152,512]{1,0:T(8,128)}) %all-reduce.5.cloned.1.call-update) | async-done | bytes 2359312 | tf_op jit(solution)/shard_map/psum | solution.py:78
  361.4 2.2 fusion.87
  363.6 0.8 fusion.89
  364.4 0.8 fusion.91
  365.2 0.9 fusion.93
  366.1 0.8 fusion.95
  366.8 52.5 %all-reduce.7.cloned.1.call-done = f32[1152,512]{1,0:T(8,128)} async-done(((f32[1152,512]{1,0:T(8,128)}), f32[1152,512]{1,0:T(8,128)}) %all-reduce.7.cloned.1.call-update) | async-done | bytes 2359312 | tf_op jit(solution)/shard_map/psum | solution.py:78
  419.3 7.9 %add_divide_fusion = (f32[1152,512]{1,0:T(8,128)}, f32[1152,512]{1,0:T(8,128)}, f32[1152,512]{1,0:T(8,128)}, f32[1152,512]{1,0:T(8,128)}) fusion(f32[1152,512]{1,0:T(8,128)} %all-reduce.7.cloned.1.call-done, f32[1152,512]{1,0:T(8,128)} %param.11, f32[1152,512]{1,0:T(8,128)} %param.10), kind=kLoop, calls=%fused_computation.14 | loop fusion | flops 5898240 | bytes 16515072 | tf_op jit(solution)/shard_map/div | solution.py:82
  (44 shorter events, 2.8 us)
Async XLA Ops:
  7.2 6.7 %copy-start.13 = (bf16[1,8,32,512]{3,2,1,0:T(8,128)(2,1)S(1)}, bf16[1,8,32,512]{3,2,1,0:T(8,128)(2,1)}, u32[]{:S(2)}) copy-start(bf16[1,8,32,512]{3,2,1,0:T(8,128)(2,1)} %param.7) | copy-start | bytes 786436
  7.2 192.3 %reduce-scatter.2.cloned.1.call-start = ((), (), s32[]{:S(2)}) async-start(), calls=%async_computation.2 | async-start | bytes 11796480 | tf_op jit(solution)/shard_map/reduce_scatter | solution.py:77
  7.2 6.6 %copy-start.3 = (bf16[6,1,8,32,512]{4,3,2,1,0:T(8,128)(2,1)S(1)}, bf16[6,1,8,32,512]{4,3,2,1,0:T(8,128)(2,1)}, u32[]{:S(2)}) copy-start(bf16[6,1,8,32,512]{4,3,2,1,0:T(8,128)(2,1)} %param.6) | copy-start | bytes 4718596
  8.4 4.4 %collective-permute-start.3 = (bf16[7,1,1,32,512]{4,3,2,1,0:T(8,128)(2,1)S(1)}, bf16[7,1,1,32,512]{4,3,2,1,0:T(8,128)(2,1)S(1)}, u32[]{:S(2)}, u32[]{:S(2)}) collective-permute-start(bf16[7,1,1,32,512]{4,3,2,1,0:T(8,128)(2,1)S(1)} %get-tuple-element.28), channel_id=1, source_target_pairs={{2,0},{4,2},{6,4},{3,1},{5,3},{7,5},{10,8},{12,10},{14,12},{11,9},... | collective-permute-start | bytes 688136 | tf_op jit(solution)/shard_map/ppermute | solution.py:16
  9.7 4.1 collective-permute-start.2
  19.9 1.4 copy-start
  31.5 260.4 %all-gather.2.cloned.1.call-start = ((), (), s32[]{:S(2)}) async-start(), calls=%async_computation.1 | async-start | bytes 5898240 | tf_op jit(solution)/shard_map/all_gather | solution.py:31
  34.4 326.9 %all-reduce.5.cloned.1.call-start = ((), (), s32[]{:S(2)}) async-start(), calls=%async_computation.3 | async-start | bytes 4718592 | tf_op jit(solution)/shard_map/psum | solution.py:78
  35.5 8.4 %collective-permute-start.1 = (bf16[6,1,1,32,512]{4,3,2,1,0:T(8,128)(2,1)S(1)}, bf16[6,1,1,32,512]{4,3,2,1,0:T(8,128)(2,1)S(1)}, u32[]{:S(2)}, u32[]{:S(2)}) collective-permute-start(bf16[6,1,1,32,512]{4,3,2,1,0:T(8,128)(2,1)S(1)} %get-tuple-element.30), channel_id=1, source_target_pairs={{2,0},{4,2},{6,4},{3,1},{5,3},{7,5},{10,8},{12,10},{14,12},{11,9},... | collective-permute-start | bytes 589832 | tf_op jit(solution)/shard_map/ppermute | solution.py:16
  36.8 8.0 %collective-permute-start = (bf16[6,1,1,32,512]{4,3,2,1,0:T(8,128)(2,1)S(1)}, bf16[6,1,1,32,512]{4,3,2,1,0:T(8,128)(2,1)S(1)}, u32[]{:S(2)}, u32[]{:S(2)}) collective-permute-start(bf16[6,1,1,32,512]{4,3,2,1,0:T(8,128)(2,1)S(1)} %get-tuple-element.29), channel_id=1, source_target_pairs={{0,2},{2,4},{4,6},{1,3},{3,5},{5,7},{8,10},{10,12},{12,14},{9,11},... | collective-permute-start | bytes 589832 | tf_op jit(solution)/shard_map/ppermute | solution.py:15
  47.2 1.7 copy-start.1
  199.5 219.8 %all-reduce.7.cloned.1.call-start = ((), (), s32[]{:S(2)}) async-start(), calls=%async_computation.4 | async-start | bytes 4718592 | tf_op jit(solution)/shard_map/psum | solution.py:78
  317.5 1.1 copy-start.5
  317.5 1.3 copy-start.7
  317.5 1.5 copy-start.8
  317.5 1.7 copy-start.9
  317.5 1.8 copy-start.10
  317.6 2.0 copy-start.11
  319.6 1.7 copy-start.2
  361.3 2.3 copy-start.4
  361.3 3.0 copy-start.12
  361.4 3.8 copy-start.6
Sparse Core Ops, SparseCore 0:
  31.6 167.7 reduce-scatter.1
  201.6 90.2 all-gather.1
  294.2 67.0 all-reduce.4
  363.7 55.6 all-reduce.6
